TPU v7x, 256 devices: a whole 4x4x8 slice. The times are simulated.
256 devices in a mesh: segment: 2 (over core), ctx: 64 (over x, z, y_hi), tp: 2 (over y_lo).
Axes of the slice: x: 4, y: 4 (y_hi: 2, y_lo: 2; y = y_hi * 2 + y_lo), z: 8, core: 2. Of those that a mesh axis runs over, the one named last changes fastest.
Arguments:
- queries: bfloat16 [8192, 32, 128], P('ctx', 'tp'), may hold values from -14 to 14
- keys: bfloat16 [8192, 8, 128], P('ctx', 'tp'), may hold values from -10 to 10
- values: bfloat16 [8192, 8, 128], P('ctx', 'tp'), may hold values from -6 to 6
- layer_in: bfloat16 [8192, 4096], P('ctx', 'tp'), may hold values from -6 to 6
- w_bc: bfloat16 [1, 4096, 1024], P(None, 'tp'), may hold values from -0.09375 to 0.09375
- w_dt: bfloat16 [1, 4096, 64], P(None, 'tp'), may hold values from -0.09375 to 0.09375
- dt_bias: float32 [1, 64], P(None, 'tp'), may hold values from -1 to 1
- decay_rate: float32 [1, 64], P(None, 'tp'), may hold values from 1.2207031e-05 to 0.06
- skip_gain: float32 [1, 64], P(None, 'tp'), may hold values from 0.5 to 2
- out_gain: float32 [1, 64, 64], P(None, 'tp'), may hold values from 0.5 to 1.5
Outputs:
- section_out: bfloat16 [2, 8192, 4096], P('segment', 'ctx', 'tp')
All inputs are finite; a program needn't handle non-finite values.
Results may differ from a plain program's by a relative error of at most 0.002.
Values may be sent and summed in bfloat16 or wider, within the bound.
No kernel may reach another device: no remote copies, remote signals or barrier semaphores. Data moves between devices by JAX's collectives and lax.ppermute only.
A program may use at most 256 MiB of HBM per device.

v0:
```python
import math
import jax
import jax.numpy as jnp
from jax import lax
from jax.sharding import PartitionSpec as P

GROUPS = 4
STATE = 128
EPSILON = 1e-05


def shifted_up(value, axis, distance):
    size = lax.axis_size(axis)
    pairs = [(source, source + distance) for source in range(size - distance)]
    return lax.ppermute(value, axis, pairs)


def swapped(value, axis):
    return lax.ppermute(value, axis, [(0, 1), (1, 0)])


def span_terms(normed, b_rows, c_rows, step_sizes, rate_row, skip_row):
    count_rows, head_count, head_width = normed.shape
    group_count = b_rows.shape[1]
    per_group = head_count // group_count
    state_root = math.sqrt(b_rows.shape[2])
    log_decay = jnp.cumsum(-step_sizes * rate_row[None, :], axis=0)
    lower_mask = jnp.arange(count_rows)[:, None] >= jnp.arange(count_rows)[None, :]
    intersection = (
        jnp.einsum("tgn,sgn->gts", c_rows, b_rows, precision=lax.Precision.HIGHEST) / state_root
    )
    log_gaps = log_decay.T[:, :, None] - log_decay.T[:, None, :]
    decays = jnp.where(lower_mask[None], jnp.exp(jnp.where(lower_mask[None], log_gaps, 0.0)), 0.0)
    mixing = (
        decays.reshape(group_count, per_group, count_rows, count_rows)
        * intersection[:, None]
        * step_sizes.T.reshape(group_count, per_group, 1, count_rows)
    )
    grouped = normed.reshape(count_rows, group_count, per_group, head_width)
    local_part = jnp.einsum(
        "gkts,sgkp->tgkp", mixing, grouped, precision=lax.Precision.HIGHEST
    ).reshape(count_rows, head_count, head_width)
    tail_weight = jnp.exp(log_decay[-1][None, :] - log_decay) * step_sizes
    weighted = (normed * tail_weight[:, :, None]).reshape(
        count_rows, group_count, per_group, head_width
    )
    ending = jnp.einsum(
        "sgkp,sgn->gkpn", weighted, b_rows, precision=lax.Precision.HIGHEST
    ).reshape(head_count, head_width, b_rows.shape[2])
    return (
        log_decay,
        local_part + skip_row[None, :, None] * normed,
        ending,
        jnp.exp(log_decay[-1]),
    )


def span_inflow(log_decay, c_rows, state_in):
    count_rows, group_count, state_n = c_rows.shape
    head_count, head_width = (state_in.shape[0], state_in.shape[1])
    per_group = head_count // group_count
    state_root = math.sqrt(state_n)
    inflow = jnp.einsum(
        "tgn,gkpn->tgkp",
        c_rows,
        state_in.reshape(group_count, per_group, head_width, state_n),
        precision=lax.Precision.HIGHEST,
    )
    return (
        jnp.exp(log_decay)[:, :, None]
        * inflow.reshape(count_rows, head_count, head_width)
        / state_root
    )


def merge_states(earlier, later):
    return (earlier[0] * later[0], later[0][:, None, None] * earlier[1] + later[1])


def exclusive_scan(decay, state, axis):
    place = lax.axis_index(axis)
    size = lax.axis_size(axis)
    incl = (decay, state)
    excl = (jnp.ones_like(decay), jnp.zeros_like(state))
    distance = 1
    while distance < size:
        got = jax.tree.map(lambda a: shifted_up(a, axis, distance), incl)
        present = place >= distance
        got = (jnp.where(present, got[0], 1.0), jnp.where(present, got[1], 0.0))
        excl = merge_states(got, excl)
        if distance * 2 < size:
            incl = merge_states(got, incl)
        distance *= 2
    return excl


def attention_half(queries, keys, values, first_row):
    row_count, q_heads, head_width = queries.shape
    kv_heads = keys.shape[1]
    group_size = q_heads // kv_heads
    score_scale = 1.0 / math.sqrt(head_width)
    last_row = first_row + row_count - 1
    query_place = first_row + jnp.arange(row_count, dtype=jnp.int32)
    grouped = queries.reshape(row_count, kv_heads, group_size, head_width).transpose(1, 2, 0, 3)
    both = jnp.concatenate([keys, values], axis=1)
    both_all = lax.all_gather(both, "ctx", axis=0, tiled=True)
    key_count = both_all.shape[0]
    block_size = math.gcd(key_count, 1024)

    def add_block(block_index, carried):
        row_top, row_total, row_sum = carried
        block_start = block_index * block_size
        block = lax.dynamic_slice_in_dim(both_all, block_start, block_size, 0)
        key_block = block[:, :kv_heads]
        value_block = block[:, kv_heads:]
        scores = (
            jnp.einsum("kgqd,skd->kgqs", grouped, key_block, preferred_element_type=jnp.float32)
            * score_scale
        )
        key_place = block_start + jnp.arange(block_size, dtype=jnp.int32)
        allowed = (query_place[:, None] >= key_place[None, :])[None, None]
        masked = jnp.where(allowed, scores, -1e30)
        new_top = jnp.maximum(row_top, jnp.max(masked, axis=3))
        raw_weight = jnp.where(allowed, jnp.exp(masked - new_top[..., None]), 0.0)
        factor = jnp.exp(row_top - new_top)
        new_total = row_total * factor + jnp.sum(raw_weight, axis=3)
        block_sum = jnp.einsum(
            "kgqs,skd->kgqd",
            raw_weight.astype(jnp.bfloat16),
            value_block,
            preferred_element_type=jnp.float32,
        )
        return (new_top, new_total, row_sum * factor[..., None] + block_sum)

    initial = (
        jnp.full((kv_heads, group_size, row_count), -1e30, jnp.float32),
        jnp.zeros((kv_heads, group_size, row_count), jnp.float32),
        jnp.zeros((kv_heads, group_size, row_count, head_width), jnp.float32),
    )
    block_count = last_row // block_size + 1
    row_top, row_total, row_sum = lax.fori_loop(0, block_count, add_block, initial)
    mixed_out = row_sum / row_total[..., None]
    return (
        mixed_out.transpose(2, 0, 1, 3)
        .reshape(row_count, q_heads * head_width)
        .astype(jnp.bfloat16)
    )


def body(queries, keys, values, layer_in, w_bc, w_dt, dt_bias, decay_rate, skip_gain, out_gain):
    seg = lax.axis_index("segment")
    seg_count = lax.axis_size("segment")
    tp = lax.axis_index("tp")
    tp_count = lax.axis_size("tp")
    row_count, q_heads, head_width = queries.shape
    kv_heads = keys.shape[1]
    first_row = lax.axis_index("ctx") * row_count
    q_share = q_heads // seg_count
    kv_share = kv_heads // seg_count
    q_part = lax.dynamic_slice_in_dim(queries, seg * q_share, q_share, 1)
    k_part = lax.dynamic_slice_in_dim(keys, seg * kv_share, kv_share, 1)
    v_part = lax.dynamic_slice_in_dim(values, seg * kv_share, kv_share, 1)
    attended = attention_half(q_part, k_part, v_part, first_row)
    current = layer_in
    channel_count = current.shape[1]
    heads_dev = dt_bias.shape[1]
    state_width = channel_count // heads_dev
    groups_dev = GROUPS // tp_count
    groups_core = groups_dev // seg_count
    heads_core = heads_dev // seg_count
    half_cols = GROUPS * STATE
    wide_rows = current.astype(jnp.float32)
    part_bc = jnp.dot(current, w_bc[0], preferred_element_type=jnp.float32)
    part_dt = jnp.dot(current, w_dt[0], preferred_element_type=jnp.float32)
    part_sq = jnp.sum(wide_rows * wide_rows, axis=1)

    def columns_for(tp_index):
        group_start = (tp_index * groups_dev + seg * groups_core) * STATE
        head_start = tp_index * heads_dev + seg * heads_core
        return jnp.concatenate(
            [
                lax.dynamic_slice_in_dim(part_bc, group_start, groups_core * STATE, 1),
                lax.dynamic_slice_in_dim(part_bc, half_cols + group_start, groups_core * STATE, 1),
                lax.dynamic_slice_in_dim(part_dt, head_start, heads_core, 1),
                part_sq[:, None],
            ],
            axis=1,
        )

    mine = columns_for(tp)
    theirs = columns_for(tp_count - 1 - tp)
    total = mine + swapped(theirs, "tp")
    width_bc = groups_core * STATE
    sum_b = total[:, :width_bc]
    sum_c = total[:, width_bc : 2 * width_bc]
    sum_dt = total[:, 2 * width_bc : 2 * width_bc + heads_core]
    sum_sq = total[:, 2 * width_bc + heads_core]
    inv_rms = lax.rsqrt(sum_sq / (channel_count * tp_count) + EPSILON)
    own_rows = lax.dynamic_slice_in_dim(
        wide_rows, seg * heads_core * state_width, heads_core * state_width, 1
    )
    normed = (own_rows * inv_rms[:, None]).reshape(row_count, heads_core, state_width)
    b_rows = (sum_b * inv_rms[:, None]).reshape(row_count, groups_core, STATE)
    c_rows = (sum_c * inv_rms[:, None]).reshape(row_count, groups_core, STATE)
    bias = lax.dynamic_slice_in_dim(dt_bias[0], seg * heads_core, heads_core, 0)
    rate = lax.dynamic_slice_in_dim(decay_rate[0], seg * heads_core, heads_core, 0)
    skip = lax.dynamic_slice_in_dim(skip_gain[0], seg * heads_core, heads_core, 0)
    gain = lax.dynamic_slice_in_dim(out_gain[0], seg * heads_core, heads_core, 0)
    step_sizes = jax.nn.softplus(sum_dt * inv_rms[:, None] + bias[None, :])
    log_decay, local_part, ending, span_decay = span_terms(
        normed, b_rows, c_rows, step_sizes, rate, skip
    )
    _, state_in = exclusive_scan(span_decay, ending, "ctx")
    mixed_out = local_part + span_inflow(log_decay, c_rows, state_in)
    power = jnp.mean(mixed_out * mixed_out, axis=2, keepdims=True)
    result = own_rows.reshape(row_count, heads_core, state_width) + gain[
        None
    ] * mixed_out * lax.rsqrt(power + EPSILON)
    state_part = result.reshape(row_count, heads_core * state_width).astype(jnp.bfloat16)
    keep_state = seg == 0
    outgoing = jnp.where(keep_state, attended, state_part)
    incoming = swapped(outgoing, "segment")
    first = jnp.where(keep_state, state_part, incoming)
    second = jnp.where(keep_state, incoming, attended)
    return jnp.concatenate([first, second], axis=1)[None]


def solution(mesh):
    in_specs = (
        P("ctx", "tp", None),
        P("ctx", "tp", None),
        P("ctx", "tp", None),
        P("ctx", "tp"),
        P(None, "tp", None),
        P(None, "tp", None),
        P(None, "tp"),
        P(None, "tp"),
        P(None, "tp"),
        P(None, "tp", None),
    )
    out_specs = P("segment", "ctx", "tp")
    return jax.shard_map(body, mesh=mesh, in_specs=in_specs, out_specs=out_specs, check_vma=False)
```

profile of v0, /device:TPU:239, one launch (start us, length us, event | category | flops | bytes accessed | tf_op | source)
XLA Modules:
  0.0 272.6 jit_solution(10316998573162825746)
XLA Ops:
  11.2 4.1 %fusion.17 = f32[128,1024]{0,1:T(8,128)S(1)} fusion(bf16[128,2048]{1,0:T(8,128)(2,1)} %param.15, bf16[1,2048,1024]{2,1,0:T(8,128)(2,1)} %param.16), kind=kOutput, calls=%fused_computation.22 | convolution fusion | flops 536870912 | bytes 5242880 | tf_op jit(solution)/shard_map/dot_general | solution.py:173
  16.1 4.3 %collective-permute-done = f32[128,273]{0,1:T(8,128)S(1)} collective-permute-done((f32[128,273]{0,1:T(8,128)S(1)}, f32[128,273]{0,1:T(8,128)S(1)}, u32[]{:S(2)}, u32[]{:S(2)}) %collective-permute-start) | collective-permute-done | bytes 139808 | tf_op jit(solution)/shard_map/ppermute | solution.py:19
  22.2 3.9 %collective-permute-start.6 = (f32[16,64,128]{2,1,0:T(8,128)S(1)}, f32[16,64,128]{2,1,0:T(8,128)}, u32[]{:S(2)}, u32[]{:S(2)}) collective-permute-start(f32[16,64,128]{2,1,0:T(8,128)S(1)} %fusion.76), channel_id=1, source_target_pairs={{0,2},{2,4},{4,6},{6,8},{8,10},{10,12},{12,14},{14,16},{16,18},{18... | collective-permute-start | bytes 1572872 | tf_op jit(solution)/shard_map/ppermute | solution.py:15
  26.2 14.1 %collective-permute-done.6 = f32[16,64,128]{2,1,0:T(8,128)} collective-permute-done((f32[16,64,128]{2,1,0:T(8,128)S(1)}, f32[16,64,128]{2,1,0:T(8,128)}, u32[]{:S(2)}, u32[]{:S(2)}) %collective-permute-start.6) | collective-permute-done | bytes 524320 | tf_op jit(solution)/shard_map/ppermute | solution.py:15
  44.7 9.4 %collective-permute-done.1 = f32[16]{0:T(128)S(1)} collective-permute-done((f32[16]{0:T(128)S(1)}, f32[16]{0:T(128)S(1)}, u32[]{:S(2)}, u32[]{:S(2)}) %collective-permute-start.1) | collective-permute-done | bytes 96 | tf_op jit(solution)/shard_map/ppermute | solution.py:15
  59.8 3.1 %collective-permute-done.2 = f32[16]{0:T(128)S(1)} collective-permute-done((f32[16]{0:T(128)}, f32[16]{0:T(128)S(1)}, u32[]{:S(2)}, u32[]{:S(2)}) %collective-permute-start.2) | collective-permute-done | bytes 96 | tf_op jit(solution)/shard_map/ppermute | solution.py:15
  63.6 23.5 %collective-permute-done.8 = f32[16,64,128]{2,1,0:T(8,128)S(1)} collective-permute-done((f32[16,64,128]{2,1,0:T(8,128)S(1)}, f32[16,64,128]{2,1,0:T(8,128)S(1)}, u32[]{:S(2)}, u32[]{:S(2)}) %collective-permute-start.8) | collective-permute-done | bytes 524320 | tf_op jit(solution)/shard_map/ppermute | solution.py:15
  91.1 6.9 %collective-permute-done.3 = f32[16]{0:T(128)S(1)} collective-permute-done((f32[16]{0:T(128)}, f32[16]{0:T(128)S(1)}, u32[]{:S(2)}, u32[]{:S(2)}) %collective-permute-start.3) | collective-permute-done | bytes 96 | tf_op jit(solution)/shard_map/ppermute | solution.py:15
  98.7 6.3 %collective-permute-done.9 = f32[16,64,128]{2,1,0:T(8,128)} collective-permute-done((f32[16,64,128]{2,1,0:T(8,128)S(1)}, f32[16,64,128]{2,1,0:T(8,128)}, u32[]{:S(2)}, u32[]{:S(2)}) %collective-permute-start.9) | collective-permute-done | bytes 524320 | tf_op jit(solution)/shard_map/ppermute | solution.py:15
  115.4 7.6 %collective-permute-done.4 = f32[16]{0:T(128)} collective-permute-done((f32[16]{0:T(128)}, f32[16]{0:T(128)}, u32[]{:S(2)}, u32[]{:S(2)}) %collective-permute-start.4) | collective-permute-done | bytes 96 | tf_op jit(solution)/shard_map/ppermute | solution.py:15
  124.7 1.9 multiply_add_fusion.1
  130.0 3.0 %fusion.19 = f32[16,64,128]{2,1,0:T(8,128)S(1)} fusion(f32[128,16,64]{0,2,1:T(8,128)S(1)} %bitcast.158, f32[16,128]{1,0:T(8,128)} %get-tuple-element.107, f32[128,128]{1,0:T(8,128)S(1)} %convolution_multiply_fusion, f32[16,128]{1,0:T(8,128)S(1)} %copy.52, pred[128,128]{1,0:T(8,128)(4,1)} %iota_compare_fusion), kind=kOutput, calls=%fused_computation.25 | convolution fusion | flops 202637312 | bytes 1146880 | tf_op jit(solution)/shard_map/gkts,sgkp->tgkp/dot_general | solution.py:40
  134.4 11.9 %collective-permute-done.5 = f32[16]{0:T(128)S(1)} collective-permute-done((f32[16]{0:T(128)}, f32[16]{0:T(128)S(1)}, u32[]{:S(2)}, u32[]{:S(2)}) %collective-permute-start.5) | collective-permute-done | bytes 96 | tf_op jit(solution)/shard_map/ppermute | solution.py:15
  148.6 3.4 %fusion.29 = (f32[128,16]{0,1:T(8,128)S(1)}, f32[16,64,128]{2,1,0:T(8,128)}) fusion(f32[16,64,128]{2,1,0:T(8,128)S(1)} %fusion.19, f32[16]{0:T(128)} %copy-done.14, f32[128,16]{0,1:T(8,128)S(1)} %copy.54, f32[128,1024]{0,1:T(8,128)S(1)} %get-tuple-element.98, f32[128,273]{0,1:T(8,128)} %copy-done.6, f32[128]{0:T(128)S(1)} %fusion.88, ...), kind=kOutput, calls=%fused_computation.38 | convolution fusion | flops 204355584 | bytes 4802310 | tf_op jit(solution)/shard_map/tgn,gkpn->tgkp/dot_general | solution.py:63
  152.6 33.1 %all-gather.2.cloned.1.call-done = bf16[8192,4,128]{2,0,1:T(8,128)(2,1)} async-done(((bf16[128,4,128]{2,0,1:T(8,128)(2,1)}), bf16[8192,4,128]{2,0,1:T(8,128)(2,1)}) %all-gather.2.cloned.1.call-update) | async-done | bytes 8388624 | tf_op jit(solution)/shard_map/all_gather | solution.py:106
  185.8 72.2 %while.15 = (s32[]{:T(128)}, f32[2,4,128]{2,1,0:T(4,128)S(1)}, f32[2,4,128]{2,1,0:T(4,128)S(1)}, f32[2,4,128,128]{3,2,1,0:T(8,128)S(1)}, s32[]{:T(128)}, /*index...) while((s32[]{:T(128)}, f32[2,4,128]{2,1,0:T(4,128)S(1)}, ...), condition=%wide.region_6.7_spmd.clone, body=%wide.region_3.6_spmd.clone.sunk | while | flops 550898816 | bytes 32318704 | solution.py:141
  188.1 2.0 copy-done.1
  191.2 3.9 %fusion.118 = f32[2,4,128,128]{3,2,1,0:T(8,128)S(1)} fusion(f32[2,1024,4,128]{3,1,2,0:T(8,128)} %copy-done.1, f32[2,4,128]{2,1,0:T(4,128)S(1)} %max.29, pred[128,1024]{0,1:T(8,128)(4,1)S(1)} %broadcast_compare_fusion.2, bf16[8192,4,128]{2,0,1:T(8,128)(2,1)} %get-tuple-element.210, s32[]{:T(128)S(6)} %select_n.373, s32[]{:T(128)S(6)} %add.345, ...), kind=kOutput, calls=%fused_computation.8.clone.1 | convolution fusion | flops 273940480 | bytes 5906440 | tf_op jit(solution)/shard_map/while/body/kgqs,skd->kgqd/dot_general | solution.py:127
  197.1 2.0 copy-done.1
  200.2 3.9 %fusion.118 = f32[2,4,128,128]{3,2,1,0:T(8,128)S(1)} fusion(f32[2,1024,4,128]{3,1,2,0:T(8,128)} %copy-done.1, f32[2,4,128]{2,1,0:T(4,128)S(1)} %max.29, pred[128,1024]{0,1:T(8,128)(4,1)S(1)} %broadcast_compare_fusion.2, bf16[8192,4,128]{2,0,1:T(8,128)(2,1)} %get-tuple-element.210, s32[]{:T(128)S(6)} %select_n.373, s32[]{:T(128)S(6)} %add.345, ...), kind=kOutput, calls=%fused_computation.8.clone.1 | convolution fusion | flops 273940480 | bytes 5906440 | tf_op jit(solution)/shard_map/while/body/kgqs,skd->kgqd/dot_general | solution.py:127
  206.1 2.0 copy-done.1
  209.2 3.9 %fusion.118 = f32[2,4,128,128]{3,2,1,0:T(8,128)S(1)} fusion(f32[2,1024,4,128]{3,1,2,0:T(8,128)} %copy-done.1, f32[2,4,128]{2,1,0:T(4,128)S(1)} %max.29, pred[128,1024]{0,1:T(8,128)(4,1)S(1)} %broadcast_compare_fusion.2, bf16[8192,4,128]{2,0,1:T(8,128)(2,1)} %get-tuple-element.210, s32[]{:T(128)S(6)} %select_n.373, s32[]{:T(128)S(6)} %add.345, ...), kind=kOutput, calls=%fused_computation.8.clone.1 | convolution fusion | flops 273940480 | bytes 5906440 | tf_op jit(solution)/shard_map/while/body/kgqs,skd->kgqd/dot_general | solution.py:127
  215.1 2.0 copy-done.1
  218.2 3.9 %fusion.118 = f32[2,4,128,128]{3,2,1,0:T(8,128)S(1)} fusion(f32[2,1024,4,128]{3,1,2,0:T(8,128)} %copy-done.1, f32[2,4,128]{2,1,0:T(4,128)S(1)} %max.29, pred[128,1024]{0,1:T(8,128)(4,1)S(1)} %broadcast_compare_fusion.2, bf16[8192,4,128]{2,0,1:T(8,128)(2,1)} %get-tuple-element.210, s32[]{:T(128)S(6)} %select_n.373, s32[]{:T(128)S(6)} %add.345, ...), kind=kOutput, calls=%fused_computation.8.clone.1 | convolution fusion | flops 273940480 | bytes 5906440 | tf_op jit(solution)/shard_map/while/body/kgqs,skd->kgqd/dot_general | solution.py:127
  224.1 2.0 copy-done.1
  227.2 3.9 %fusion.118 = f32[2,4,128,128]{3,2,1,0:T(8,128)S(1)} fusion(f32[2,1024,4,128]{3,1,2,0:T(8,128)} %copy-done.1, f32[2,4,128]{2,1,0:T(4,128)S(1)} %max.29, pred[128,1024]{0,1:T(8,128)(4,1)S(1)} %broadcast_compare_fusion.2, bf16[8192,4,128]{2,0,1:T(8,128)(2,1)} %get-tuple-element.210, s32[]{:T(128)S(6)} %select_n.373, s32[]{:T(128)S(6)} %add.345, ...), kind=kOutput, calls=%fused_computation.8.clone.1 | convolution fusion | flops 273940480 | bytes 5906440 | tf_op jit(solution)/shard_map/while/body/kgqs,skd->kgqd/dot_general | solution.py:127
  233.1 2.0 copy-done.1
  236.2 3.9 %fusion.118 = f32[2,4,128,128]{3,2,1,0:T(8,128)S(1)} fusion(f32[2,1024,4,128]{3,1,2,0:T(8,128)} %copy-done.1, f32[2,4,128]{2,1,0:T(4,128)S(1)} %max.29, pred[128,1024]{0,1:T(8,128)(4,1)S(1)} %broadcast_compare_fusion.2, bf16[8192,4,128]{2,0,1:T(8,128)(2,1)} %get-tuple-element.210, s32[]{:T(128)S(6)} %select_n.373, s32[]{:T(128)S(6)} %add.345, ...), kind=kOutput, calls=%fused_computation.8.clone.1 | convolution fusion | flops 273940480 | bytes 5906440 | tf_op jit(solution)/shard_map/while/body/kgqs,skd->kgqd/dot_general | solution.py:127
  242.2 2.0 copy-done.1
  245.2 3.9 %fusion.118 = f32[2,4,128,128]{3,2,1,0:T(8,128)S(1)} fusion(f32[2,1024,4,128]{3,1,2,0:T(8,128)} %copy-done.1, f32[2,4,128]{2,1,0:T(4,128)S(1)} %max.29, pred[128,1024]{0,1:T(8,128)(4,1)S(1)} %broadcast_compare_fusion.2, bf16[8192,4,128]{2,0,1:T(8,128)(2,1)} %get-tuple-element.210, s32[]{:T(128)S(6)} %select_n.373, s32[]{:T(128)S(6)} %add.345, ...), kind=kOutput, calls=%fused_computation.8.clone.1 | convolution fusion | flops 273940480 | bytes 5906440 | tf_op jit(solution)/shard_map/while/body/kgqs,skd->kgqd/dot_general | solution.py:127
  251.2 2.0 copy-done.1
  254.2 3.9 %fusion.118 = f32[2,4,128,128]{3,2,1,0:T(8,128)S(1)} fusion(f32[2,1024,4,128]{3,1,2,0:T(8,128)} %copy-done.1, f32[2,4,128]{2,1,0:T(4,128)S(1)} %max.29, pred[128,1024]{0,1:T(8,128)(4,1)S(1)} %broadcast_compare_fusion.2, bf16[8192,4,128]{2,0,1:T(8,128)(2,1)} %get-tuple-element.210, s32[]{:T(128)S(6)} %select_n.373, s32[]{:T(128)S(6)} %add.345, ...), kind=kOutput, calls=%fused_computation.8.clone.1 | convolution fusion | flops 273940480 | bytes 5906440 | tf_op jit(solution)/shard_map/while/body/kgqs,skd->kgqd/dot_general | solution.py:127
  (176 shorter events, 74.4 us)
Async XLA Ops:
  6.5 83.2 %copy-start = (bf16[128,16,128]{2,1,0:T(8,128)(2,1)S(1)}, bf16[128,16,128]{2,1,0:T(8,128)(2,1)}, u32[]{:S(2)}) copy-start(bf16[128,16,128]{2,1,0:T(8,128)(2,1)} %param.12) | copy-start | bytes 1572868
  6.5 179.3 %all-gather.2.cloned.1.call-start = ((), (), s32[]{:S(2)}) async-start(), calls=%async_computation | async-start | bytes 8519680 | tf_op jit(solution)/shard_map/all_gather | solution.py:106
  11.2 4.8 %copy-start.15 = (f32[1,32]{1,0:T(1,128)S(1)}, f32[1,32]{1,0:T(1,128)}, u32[]{:S(2)}) copy-start(f32[1,32]{1,0:T(1,128)} %param.18) | copy-start | bytes 388
  11.2 4.8 %copy-start.16 = (f32[1,32]{1,0:T(1,128)S(1)}, f32[1,32]{1,0:T(1,128)}, u32[]{:S(2)}) copy-start(f32[1,32]{1,0:T(1,128)} %param.19) | copy-start | bytes 388
  15.7 4.7 %collective-permute-start = (f32[128,273]{0,1:T(8,128)S(1)}, f32[128,273]{0,1:T(8,128)S(1)}, u32[]{:S(2)}, u32[]{:S(2)}) collective-permute-start(f32[128,273]{0,1:T(8,128)S(1)} %pad_maximum_fusion), channel_id=1, source_target_pairs={{0,1},{1,0},{2,3},{3,2},{4,5},{5,4},{6,7},{7,6},{8,9},{9,8},{10,11... | collective-permute-start | bytes 419336 | tf_op jit(solution)/shard_map/ppermute | solution.py:19
  20.4 107.5 %copy-start.6 = (f32[128,273]{0,1:T(8,128)}, f32[128,273]{0,1:T(8,128)S(1)}, u32[]{:S(2)}) copy-start(f32[128,273]{0,1:T(8,128)S(1)} %fusion.74) | copy-start | bytes 419332
  20.8 35.2 %copy-start.7 = (f32[128,16]{1,0:T(8,128)}, f32[128,16]{1,0:T(8,128)S(1)}, u32[]{:S(2)}) copy-start(f32[128,16]{1,0:T(8,128)S(1)} %reduce_window_sum.11) | copy-start | bytes 24580
  22.2 18.1 %collective-permute-start.6 = (f32[16,64,128]{2,1,0:T(8,128)S(1)}, f32[16,64,128]{2,1,0:T(8,128)}, u32[]{:S(2)}, u32[]{:S(2)}) collective-permute-start(f32[16,64,128]{2,1,0:T(8,128)S(1)} %fusion.76), channel_id=1, source_target_pairs={{0,2},{2,4},{4,6},{6,8},{8,10},{10,12},{12,14},{14,16},{16,18},{18... | collective-permute-start | bytes 1572872 | tf_op jit(solution)/shard_map/ppermute | solution.py:15
  41.5 13.8 %collective-permute-start.7 = (f32[16,64,128]{2,1,0:T(8,128)S(1)}, f32[16,64,128]{2,1,0:T(8,128)S(1)}, u32[]{:S(2)}, u32[]{:S(2)}) collective-permute-start(f32[16,64,128]{2,1,0:T(8,128)S(1)} %multiply_add_fusion.5), channel_id=1, source_target_pairs={{0,4},{2,6},{4,8},{6,10},{8,12},{10,14},{12,16},{14,18},{16,20},{1... | collective-permute-start | bytes 1572872 | tf_op jit(solution)/shard_map/ppermute | solution.py:15
  42.8 11.3 %collective-permute-start.1 = (f32[16]{0:T(128)S(1)}, f32[16]{0:T(128)S(1)}, u32[]{:S(2)}, u32[]{:S(2)}) collective-permute-start(f32[16]{0:T(128)S(1)} %fusion.97), channel_id=1, source_target_pairs={{0,2},{2,4},{4,6},{6,8},{8,10},{10,12},{12,14},{14,16},{16,18},{18... | collective-permute-start | bytes 200 | tf_op jit(solution)/shard_map/ppermute | solution.py:15
  57.2 6.4 %copy-start.2 = (f32[16,64,128]{2,1,0:T(8,128)}, f32[16,64,128]{2,1,0:T(8,128)S(1)}, u32[]{:S(2)}) copy-start(f32[16,64,128]{2,1,0:T(8,128)S(1)} %multiply_add_fusion.4) | copy-start | bytes 1572868
  57.2 29.8 %collective-permute-start.8 = (f32[16,64,128]{2,1,0:T(8,128)S(1)}, f32[16,64,128]{2,1,0:T(8,128)S(1)}, u32[]{:S(2)}, u32[]{:S(2)}) collective-permute-start(f32[16,64,128]{2,1,0:T(8,128)S(1)} %multiply_add_fusion.4), channel_id=1, source_target_pairs={{0,8},{2,10},{4,12},{6,14},{8,16},{10,18},{12,20},{14,22},{16,24},... | collective-permute-start | bytes 1572872 | tf_op jit(solution)/shard_map/ppermute | solution.py:15
  58.5 4.4 %collective-permute-start.2 = (f32[16]{0:T(128)}, f32[16]{0:T(128)S(1)}, u32[]{:S(2)}, u32[]{:S(2)}) collective-permute-start(f32[16]{0:T(128)} %get-tuple-element.95), channel_id=1, source_target_pairs={{0,4},{2,6},{4,8},{6,10},{8,12},{10,14},{12,16},{14,18},{16,20},{1... | collective-permute-start | bytes 200 | tf_op jit(solution)/shard_map/ppermute | solution.py:15
  63.6 23.5 %copy-start.9 = (f32[16]{0:T(128)}, f32[16]{0:T(128)S(1)}, u32[]{:S(2)}) copy-start(f32[16]{0:T(128)S(1)} %fusion.94) | copy-start | bytes 196
  87.1 11.6 %copy-start.4 = (f32[16,64,128]{2,1,0:T(8,128)}, f32[16,64,128]{2,1,0:T(8,128)S(1)}, u32[]{:S(2)}) copy-start(f32[16,64,128]{2,1,0:T(8,128)S(1)} %collective-permute-done.8) | copy-start | bytes 1572868
  88.4 16.6 %collective-permute-start.9 = (f32[16,64,128]{2,1,0:T(8,128)S(1)}, f32[16,64,128]{2,1,0:T(8,128)}, u32[]{:S(2)}, u32[]{:S(2)}) collective-permute-start(f32[16,64,128]{2,1,0:T(8,128)S(1)} %multiply_add_fusion.3), channel_id=1, source_target_pairs={{0,16},{2,18},{4,20},{6,22},{8,24},{10,26},{12,28},{14,30},{16,32}... | collective-permute-start | bytes 1572872 | tf_op jit(solution)/shard_map/ppermute | solution.py:15
  89.8 8.3 %collective-permute-start.3 = (f32[16]{0:T(128)}, f32[16]{0:T(128)S(1)}, u32[]{:S(2)}, u32[]{:S(2)}) collective-permute-start(f32[16]{0:T(128)} %copy-done.9), channel_id=1, source_target_pairs={{0,8},{2,10},{4,12},{6,14},{8,16},{10,18},{12,20},{14,22},{16,24},... | collective-permute-start | bytes 200 | tf_op jit(solution)/shard_map/ppermute | solution.py:15
  98.7 7.5 %copy-start.10 = (f32[16]{0:T(128)}, f32[16]{0:T(128)S(1)}, u32[]{:S(2)}) copy-start(f32[16]{0:T(128)S(1)} %fusion.92) | copy-start | bytes 196
  106.2 42.4 %copy-start.5 = (f32[16,64,128]{2,1,0:T(8,128)S(1)}, f32[16,64,128]{2,1,0:T(8,128)}, u32[]{:S(2)}) copy-start(f32[16,64,128]{2,1,0:T(8,128)} %copy-done.4) | copy-start | bytes 1572868
  106.2 18.5 %collective-permute-start.10 = (f32[16,64,128]{2,1,0:T(8,128)S(1)}, f32[16,64,128]{2,1,0:T(8,128)}, u32[]{:S(2)}, u32[]{:S(2)}) collective-permute-start(f32[16,64,128]{2,1,0:T(8,128)S(1)} %multiply_add_fusion.2), channel_id=1, source_target_pairs={{0,32},{2,34},{4,36},{6,38},{8,40},{10,42},{12,44},{14,46},{16,48}... | collective-permute-start | bytes 1572872 | tf_op jit(solution)/shard_map/ppermute | solution.py:15
  112.8 10.3 %collective-permute-start.4 = (f32[16]{0:T(128)}, f32[16]{0:T(128)}, u32[]{:S(2)}, u32[]{:S(2)}) collective-permute-start(f32[16]{0:T(128)} %copy-done.10), channel_id=1, source_target_pairs={{0,16},{2,18},{4,20},{6,22},{8,24},{10,26},{12,28},{14,30},{16,32}... | collective-permute-start | bytes 200 | tf_op jit(solution)/shard_map/ppermute | solution.py:15
  123.7 5.4 %copy-start.11 = (f32[16]{0:T(128)}, f32[16]{0:T(128)S(1)}, u32[]{:S(2)}) copy-start(f32[16]{0:T(128)S(1)} %fusion.90) | copy-start | bytes 196
  126.6 22.0 %collective-permute-start.11 = (f32[16,64,128]{2,1,0:T(8,128)}, f32[16,64,128]{2,1,0:T(8,128)}, u32[]{:S(2)}, u32[]{:S(2)}) collective-permute-start(f32[16,64,128]{2,1,0:T(8,128)} %multiply_add_fusion.1), channel_id=1, source_target_pairs={{0,64},{2,66},{4,68},{6,70},{8,72},{10,74},{12,76},{14,78},{16,80}... | collective-permute-start | bytes 1572872 | tf_op jit(solution)/shard_map/ppermute | solution.py:15
  133.0 13.3 %collective-permute-start.5 = (f32[16]{0:T(128)}, f32[16]{0:T(128)S(1)}, u32[]{:S(2)}, u32[]{:S(2)}) collective-permute-start(f32[16]{0:T(128)} %copy-done.11), channel_id=1, source_target_pairs={{0,32},{2,34},{4,36},{6,38},{8,40},{10,42},{12,44},{14,46},{16,48}... | collective-permute-start | bytes 200 | tf_op jit(solution)/shard_map/ppermute | solution.py:15
  134.3 51.5 %copy-start.8 = (f32[128,16]{0,1:T(8,128)}, f32[128,16]{0,1:T(8,128)S(1)}, u32[]{:S(2)}) copy-start(f32[128,16]{0,1:T(8,128)S(1)} %copy.54) | copy-start | bytes 24580
  188.1 2.0 copy-start.1
  197.1 2.0 copy-start.1
  206.1 2.0 copy-start.1
  215.1 2.0 copy-start.1
  224.1 2.0 copy-start.1
  242.1 2.0 copy-start.1
  261.5 3.1 %collective-permute-start.12 = (bf16[128,1024]{0,1:T(8,128)(2,1)S(1)}, bf16[128,1024]{0,1:T(8,128)(2,1)S(1)}, u32[]{:S(2)}, u32[]{:S(2)}) collective-permute-start(bf16[128,1024]{0,1:T(8,128)(2,1)S(1)} %get-tuple-element.89), channel_id=1, source_target_pairs={{0,128},{128,0},{1,129},{129,1},{2,130},{130,2},{3,131},{131,3},{4... | collective-permute-start | bytes 786440 | tf_op jit(solution)/shard_map/ppermute | solution.py:19
  (6 other events, 6.5 us)
Sparse Core Ops, SparseCore 0:
  10.9 174.8 all-gather.1
where the time goes:
time: 274 us; the launch traced here: 273 us
  waiting for transfers between devices  125 us (46%)
  matrix products  58.2 us (21%)
  local copies, waits for them, and re-layouts  29.5 us (11%)
  other arithmetic  25.5 us (9%)
  starting transfers between devices  19.8 us (7%)
  between operations  13.8 us (5%)
    ppermute x11, waiting for transfers between devices, shifted_up(): return lax.ppermute(value, axis, pairs)  86.3 us
    all_gather x1, waiting for transfers between devices, attention_half(): both_all = lax.all_gather(both, 'ctx', axis=0, tiled=True)  33.1 us
    dot_general x8, matrix products, add_block(): jnp.einsum('kgqs,skd->kgqd', raw_weight.astype(jnp.bfloat16), value_block...  30.9 us
    ppermute x11, starting transfers between devices, shifted_up(): return lax.ppermute(value, axis, pairs)  17.6 us
    while x24, local copies, waits for them, and re-layouts  15.9 us
    dot_general x8, matrix products, add_block(): jnp.einsum('kgqd,skd->kgqs', grouped, key_block, preferred_element_type=j...  14.5 us
    reduce_sum x8, other arithmetic, add_block(): new_total = row_total * factor + jnp.sum(raw_weight, axis=3)  8.18 us
    add x5, other arithmetic, merge_states(): later[0][:, None, None] * earlier[1] + later[1]  6.77 us
  transfers between devices with their start and end apart: 14, of which 14 were waited for; matrix products, arithmetic and copies ran while one was open for 13% of the time, Pallas kernels for 0%

commit v1 on v0

--- a/solution.py
+++ b/solution.py
@@ -1,12 +1,23 @@
+import functools
 import math
 import jax
 import jax.numpy as jnp
 from jax import lax
 from jax.sharding import PartitionSpec as P
+from jax.lax import all_to_all, axis_size
 
 GROUPS = 4
 STATE = 128
 EPSILON = 1e-05
+
+
+def compute_leaves_all(field, dimension_no):
+    all_rows = jnp.stack([field for _ in range(axis_size("ctx"))], axis=0)
+    arr_out = all_to_all(all_rows, concat_axis=0, split_axis=0, axis_name="ctx")
+    return jnp.concatenate(arr_out, axis=dimension_no)
+
+
+serve_pairs_all = functools.partial(compute_leaves_all, dimension_no=0)
 
 
 def shifted_up(value, axis, distance):
@@ -103,7 +114,7 @@
     query_place = first_row + jnp.arange(row_count, dtype=jnp.int32)
     grouped = queries.reshape(row_count, kv_heads, group_size, head_width).transpose(1, 2, 0, 3)
     both = jnp.concatenate([keys, values], axis=1)
-    both_all = lax.all_gather(both, "ctx", axis=0, tiled=True)
+    both_all = serve_pairs_all(both)
     key_count = both_all.shape[0]
     block_size = math.gcd(key_count, 1024)
 

time: 274 us -> 420 us (1.53)
  waiting for transfers between devices: 125 us -> 272 us
  between operations: 13.8 us -> 0.46 us
  starting transfers between devices: 19.8 us -> 32.6 us
  local copies, waits for them, and re-layouts: 29.5 us -> 35.4 us
  other arithmetic: 25.5 us -> 20.5 us
    ppermute x11, waiting for transfers between devices: 86.3 us -> 253 us  [shifted_up(): return lax.ppermute(value, axis, pairs)]
    all_gather x1 -> x0, waiting for transfers between devices: 33.1 us -> none  [attention_half(): both_all = lax.all_gather(both, 'ctx', axis=0, tiled=True)]
    ppermute x2, waiting for transfers between devices: 5.47 us -> 18.9 us  [swapped(): return lax.ppermute(value, axis, [(0, 1), (1, 0)])]
    all_to_all x0 -> x1, starting transfers between devices: none -> 10.6 us  [compute_leaves_all(): arr_out = all_to_all(all_rows, concat_axis=0, split_axis=0, axis_name='ctx')]
    all_to_all x0 -> x1, local copies, waits for them, and re-layouts: none -> 10.3 us  [compute_leaves_all(): arr_out = all_to_all(all_rows, concat_axis=0, split_axis=0, axis_name='ctx')]
    another operation x0 -> x1, local copies, waits for them, and re-layouts: none -> 5.35 us  [compute_leaves_all(): all_rows = jnp.stack([field for _ in range(axis_size('ctx'))], axis=0)]
  transfers between devices with their start and end apart: 14 -> 14, of which waited for: 14 -> 13; matrix products, arithmetic and copies ran while one was open for 13% -> 5% of each run, Pallas kernels for 0% -> 0%
where the time goes in v1:
time: 420 us; the launch traced here: 418 us
  waiting for transfers between devices  272 us (65%)
  matrix products  56.3 us (13%)
  local copies, waits for them, and re-layouts  35.4 us (8%)
  starting transfers between devices  32.6 us (8%)
  other arithmetic  20.5 us (5%)
    ppermute x11, waiting for transfers between devices, shifted_up(): return lax.ppermute(value, axis, pairs)  253 us
    dot_general x8, matrix products, add_block(): jnp.einsum('kgqs,skd->kgqd', raw_weight.astype(jnp.bfloat16), value_block...  30.9 us
    ppermute x2, waiting for transfers between devices, swapped(): return lax.ppermute(value, axis, [(0, 1), (1, 0)])  18.9 us
    ppermute x11, starting transfers between devices, shifted_up(): return lax.ppermute(value, axis, pairs)  18.7 us
    while x24, local copies, waits for them, and re-layouts  15.4 us
    dot_general x8, matrix products, add_block(): jnp.einsum('kgqd,skd->kgqs', grouped, key_block, preferred_element_type=j...  14.6 us
    all_to_all x1, starting transfers between devices, compute_leaves_all(): arr_out = all_to_all(all_rows, concat_axis=0, split_axis=0, axis_name='ctx')  10.6 us
    all_to_all x1, local copies, waits for them, and re-layouts, compute_leaves_all(): arr_out = all_to_all(all_rows, concat_axis=0, split_axis=0, axis_name='ctx')  10.3 us
  transfers between devices with their start and end apart: 14, of which 13 were waited for; matrix products, arithmetic and copies ran while one was open for 5% of the time, Pallas kernels for 0%

profile of v1, /device:TPU:239, one launch (start us, length us, event | category | flops | bytes accessed | tf_op | source)
XLA Modules:
  0.0 418.3 jit_solution(1201703176398546880)
XLA Ops:
  1.3 5.3 %stack.2 = bf16[64,128,4,128]{3,1,2,0:T(8,128)(2,1)} broadcast(bf16[128,4,128]{2,0,1:T(8,128)(2,1)S(1)} %copy.87), dimensions={1,2,3} | broadcast | bytes 8519680 | tf_op jit(solution)/shard_map/stack | solution.py:15
  6.7 10.6 %all-to-all-start = ((bf16[64,128,4,128]{3,1,2,0:T(8,128)(2,1)}), bf16[64,128,4,128]{3,1,2,0:T(8,128)(2,1)}, u32[]{:S(2)}, u32[]{:S(2)}) async-start(bf16[64,128,4,128]{3,1,2,0:T(8,128)(2,1)} %stack.2), calls=%async_computation | async-start | bytes 16777216 | tf_op jit(solution)/shard_map/all_to_all | solution.py:16
  17.9 3.9 fusion.17
  23.5 17.7 %collective-permute-done = f32[128,273]{0,1:T(8,128)S(1)} collective-permute-done((f32[128,273]{0,1:T(8,128)S(1)}, f32[128,273]{0,1:T(8,128)S(1)}, u32[]{:S(2)}, u32[]{:S(2)}) %collective-permute-start) | collective-permute-done | bytes 139808 | tf_op jit(solution)/shard_map/ppermute | solution.py:30
  42.5 5.0 %collective-permute-start.6 = (f32[16,64,128]{2,1,0:T(8,128)S(1)}, f32[16,64,128]{2,1,0:T(8,128)}, u32[]{:S(2)}, u32[]{:S(2)}) collective-permute-start(f32[16,64,128]{2,1,0:T(8,128)S(1)} %fusion.76), channel_id=1, source_target_pairs={{0,2},{2,4},{4,6},{6,8},{8,10},{10,12},{12,14},{14,16},{16,18},{18... | collective-permute-start | bytes 1572872 | tf_op jit(solution)/shard_map/ppermute | solution.py:26
  47.6 165.3 %collective-permute-done.6 = f32[16,64,128]{2,1,0:T(8,128)} collective-permute-done((f32[16,64,128]{2,1,0:T(8,128)S(1)}, f32[16,64,128]{2,1,0:T(8,128)}, u32[]{:S(2)}, u32[]{:S(2)}) %collective-permute-start.6) | collective-permute-done | bytes 524320 | tf_op jit(solution)/shard_map/ppermute | solution.py:26
  217.3 8.5 %collective-permute-done.1 = f32[16]{0:T(128)S(1)} collective-permute-done((f32[16]{0:T(128)S(1)}, f32[16]{0:T(128)S(1)}, u32[]{:S(2)}, u32[]{:S(2)}) %collective-permute-start.1) | collective-permute-done | bytes 96 | tf_op jit(solution)/shard_map/ppermute | solution.py:26
  225.7 2.2 collective-permute-done.7
  232.5 3.0 collective-permute-done.2
  235.6 22.0 %collective-permute-done.8 = f32[16,64,128]{2,1,0:T(8,128)} collective-permute-done((f32[16,64,128]{2,1,0:T(8,128)S(1)}, f32[16,64,128]{2,1,0:T(8,128)}, u32[]{:S(2)}, u32[]{:S(2)}) %collective-permute-start.8) | collective-permute-done | bytes 524320 | tf_op jit(solution)/shard_map/ppermute | solution.py:26
  261.4 4.4 %collective-permute-done.3 = f32[16]{0:T(128)S(1)} collective-permute-done((f32[16]{0:T(128)S(1)}, f32[16]{0:T(128)S(1)}, u32[]{:S(2)}, u32[]{:S(2)}) %collective-permute-start.3) | collective-permute-done | bytes 96 | tf_op jit(solution)/shard_map/ppermute | solution.py:26
  265.8 10.3 %collective-permute-done.9 = f32[16,64,128]{2,1,0:T(8,128)} collective-permute-done((f32[16,64,128]{2,1,0:T(8,128)S(1)}, f32[16,64,128]{2,1,0:T(8,128)}, u32[]{:S(2)}, u32[]{:S(2)}) %collective-permute-start.9) | collective-permute-done | bytes 524320 | tf_op jit(solution)/shard_map/ppermute | solution.py:26
  276.0 2.0 multiply_add_fusion.2
  280.9 14.9 %collective-permute-done.4 = f32[16]{0:T(128)S(1)} collective-permute-done((f32[16]{0:T(128)S(1)}, f32[16]{0:T(128)S(1)}, u32[]{:S(2)}, u32[]{:S(2)}) %collective-permute-start.4) | collective-permute-done | bytes 96 | tf_op jit(solution)/shard_map/ppermute | solution.py:26
  295.8 12.4 %collective-permute-done.10 = f32[16,64,128]{2,1,0:T(8,128)S(1)} collective-permute-done((f32[16,64,128]{2,1,0:T(8,128)}, f32[16,64,128]{2,1,0:T(8,128)S(1)}, u32[]{:S(2)}, u32[]{:S(2)}) %collective-permute-start.10) | collective-permute-done | bytes 524320 | tf_op jit(solution)/shard_map/ppermute | solution.py:26
  308.3 2.1 multiply_add_fusion.1
  312.1 2.2 fusion.19
  315.9 3.2 collective-permute-done.5
  319.1 7.4 %collective-permute-done.11 = f32[16,64,128]{2,1,0:T(8,128)} collective-permute-done((f32[16,64,128]{2,1,0:T(8,128)}, f32[16,64,128]{2,1,0:T(8,128)}, u32[]{:S(2)}, u32[]{:S(2)}) %collective-permute-start.11) | collective-permute-done | bytes 524320 | tf_op jit(solution)/shard_map/ppermute | solution.py:26
  326.4 3.5 fusion.29
  329.9 10.3 %copy.88 = bf16[64,128,4,128]{3,1,0,2:T(8,128)(2,1)} copy(bf16[64,128,4,128]{3,1,2,0:T(8,128)(2,1)} %all-to-all-done) | data formatting | bytes 16777216 | tf_op jit(solution)/shard_map/all_to_all | solution.py:16
  340.3 71.5 %while.15 = (s32[]{:T(128)}, f32[2,4,128]{2,1,0:T(4,128)S(1)}, f32[2,4,128]{2,1,0:T(4,128)S(1)}, f32[2,4,128,128]{3,2,1,0:T(8,128)S(1)}, s32[]{:T(128)}, /*index...) while((s32[]{:T(128)}, f32[2,4,128]{2,1,0:T(4,128)S(1)}, ...), condition=%wide.region_6.7_spmd.clone, body=%wide.region_3.6_spmd.clone.sunk | while | flops 550898816 | bytes 32318704 | solution.py:152
  345.4 3.9 fusion.118
  354.3 3.9 fusion.118
  363.3 3.9 fusion.118
  372.2 3.9 fusion.118
  381.2 3.9 fusion.118
  387.1 1.9 copy-done.1
  390.1 3.9 fusion.118
  399.0 3.9 fusion.118
  408.0 3.9 fusion.118
  413.8 2.1 collective-permute-start.12
  (164 shorter events, 65.9 us)
Async XLA Ops:
  0.0 260.0 %copy-start = (bf16[128,16,128]{2,1,0:T(8,128)(2,1)S(1)}, bf16[128,16,128]{2,1,0:T(8,128)(2,1)}, u32[]{:S(2)}) copy-start(bf16[128,16,128]{2,1,0:T(8,128)(2,1)} %param.12) | copy-start | bytes 1572868
  6.7 10.6 %copy-start.2 = (bf16[128,2048]{1,0:T(8,128)(2,1)S(1)}, bf16[128,2048]{1,0:T(8,128)(2,1)}, u32[]{:S(2)}) copy-start(bf16[128,2048]{1,0:T(8,128)(2,1)} %param.15) | copy-start | bytes 1572868
  6.7 10.9 %copy-start.6 = (bf16[1,2048,64]{1,2,0:T(8,128)(2,1)S(1)}, bf16[1,2048,64]{1,2,0:T(8,128)(2,1)}, u32[]{:S(2)}) copy-start(bf16[1,2048,64]{1,2,0:T(8,128)(2,1)} %param.17) | copy-start | bytes 786436
  6.7 323.2 %all-to-all-start = ((bf16[64,128,4,128]{3,1,2,0:T(8,128)(2,1)}), bf16[64,128,4,128]{3,1,2,0:T(8,128)(2,1)}, u32[]{:S(2)}, u32[]{:S(2)}) async-start(bf16[64,128,4,128]{3,1,2,0:T(8,128)(2,1)} %stack.2), calls=%async_computation | async-start | bytes 16777216 | tf_op jit(solution)/shard_map/all_to_all | solution.py:16
  17.9 5.6 %copy-start.8 = (f32[1,32]{1,0:T(1,128)S(1)}, f32[1,32]{1,0:T(1,128)}, u32[]{:S(2)}) copy-start(f32[1,32]{1,0:T(1,128)} %param.18) | copy-start | bytes 388
  17.9 5.5 %copy-start.9 = (f32[1,32]{1,0:T(1,128)S(1)}, f32[1,32]{1,0:T(1,128)}, u32[]{:S(2)}) copy-start(f32[1,32]{1,0:T(1,128)} %param.19) | copy-start | bytes 388
  22.2 19.0 %collective-permute-start = (f32[128,273]{0,1:T(8,128)S(1)}, f32[128,273]{0,1:T(8,128)S(1)}, u32[]{:S(2)}, u32[]{:S(2)}) collective-permute-start(f32[128,273]{0,1:T(8,128)S(1)} %pad_maximum_fusion), channel_id=1, source_target_pairs={{0,1},{1,0},{2,3},{3,2},{4,5},{5,4},{6,7},{7,6},{8,9},{9,8},{10,11... | collective-permute-start | bytes 419336 | tf_op jit(solution)/shard_map/ppermute | solution.py:30
  41.9 237.4 %copy-start.10 = (f32[1,32]{1,0:T(1,128)S(1)}, f32[1,32]{1,0:T(1,128)}, u32[]{:S(2)}) copy-start(f32[1,32]{1,0:T(1,128)} %param.20) | copy-start | bytes 388
  41.9 237.6 %copy-start.7 = (f32[1,32,64]{2,1,0:T(8,128)S(1)}, f32[1,32,64]{2,1,0:T(8,128)}, u32[]{:S(2)}) copy-start(f32[1,32,64]{2,1,0:T(8,128)} %param.21) | copy-start | bytes 24580
  42.5 170.3 %collective-permute-start.6 = (f32[16,64,128]{2,1,0:T(8,128)S(1)}, f32[16,64,128]{2,1,0:T(8,128)}, u32[]{:S(2)}, u32[]{:S(2)}) collective-permute-start(f32[16,64,128]{2,1,0:T(8,128)S(1)} %fusion.76), channel_id=1, source_target_pairs={{0,2},{2,4},{4,6},{6,8},{8,10},{10,12},{12,14},{14,16},{16,18},{18... | collective-permute-start | bytes 1572872 | tf_op jit(solution)/shard_map/ppermute | solution.py:26
  214.0 13.9 %collective-permute-start.7 = (f32[16,64,128]{2,1,0:T(8,128)S(1)}, f32[16,64,128]{2,1,0:T(8,128)S(1)}, u32[]{:S(2)}, u32[]{:S(2)}) collective-permute-start(f32[16,64,128]{2,1,0:T(8,128)S(1)} %multiply_add_fusion.5), channel_id=1, source_target_pairs={{0,4},{2,6},{4,8},{6,10},{8,12},{10,14},{12,16},{14,18},{16,20},{1... | collective-permute-start | bytes 1572872 | tf_op jit(solution)/shard_map/ppermute | solution.py:26
  215.3 10.4 %collective-permute-start.1 = (f32[16]{0:T(128)S(1)}, f32[16]{0:T(128)S(1)}, u32[]{:S(2)}, u32[]{:S(2)}) collective-permute-start(f32[16]{0:T(128)S(1)} %fusion.97), channel_id=1, source_target_pairs={{0,2},{2,4},{4,6},{6,8},{8,10},{10,12},{12,14},{14,16},{16,18},{18... | collective-permute-start | bytes 200 | tf_op jit(solution)/shard_map/ppermute | solution.py:26
  228.0 0.8 copy-start.3
  229.9 27.6 %collective-permute-start.8 = (f32[16,64,128]{2,1,0:T(8,128)S(1)}, f32[16,64,128]{2,1,0:T(8,128)}, u32[]{:S(2)}, u32[]{:S(2)}) collective-permute-start(f32[16,64,128]{2,1,0:T(8,128)S(1)} %multiply_add_fusion.4), channel_id=1, source_target_pairs={{0,8},{2,10},{4,12},{6,14},{8,16},{10,18},{12,20},{14,22},{16,24},... | collective-permute-start | bytes 1572872 | tf_op jit(solution)/shard_map/ppermute | solution.py:26
  231.2 4.3 %collective-permute-start.2 = (f32[16]{0:T(128)S(1)}, f32[16]{0:T(128)S(1)}, u32[]{:S(2)}, u32[]{:S(2)}) collective-permute-start(f32[16]{0:T(128)S(1)} %get-tuple-element.95), channel_id=1, source_target_pairs={{0,4},{2,6},{4,8},{6,10},{8,12},{10,14},{12,16},{14,18},{16,20},{1... | collective-permute-start | bytes 200 | tf_op jit(solution)/shard_map/ppermute | solution.py:26
  258.7 17.4 %collective-permute-start.9 = (f32[16,64,128]{2,1,0:T(8,128)S(1)}, f32[16,64,128]{2,1,0:T(8,128)}, u32[]{:S(2)}, u32[]{:S(2)}) collective-permute-start(f32[16,64,128]{2,1,0:T(8,128)S(1)} %multiply_add_fusion.3), channel_id=1, source_target_pairs={{0,16},{2,18},{4,20},{6,22},{8,24},{10,26},{12,28},{14,30},{16,32}... | collective-permute-start | bytes 1572872 | tf_op jit(solution)/shard_map/ppermute | solution.py:26
  260.0 5.7 %collective-permute-start.3 = (f32[16]{0:T(128)S(1)}, f32[16]{0:T(128)S(1)}, u32[]{:S(2)}, u32[]{:S(2)}) collective-permute-start(f32[16]{0:T(128)S(1)} %fusion.94), channel_id=1, source_target_pairs={{0,8},{2,10},{4,12},{6,14},{8,16},{10,18},{12,20},{14,22},{16,24},... | collective-permute-start | bytes 200 | tf_op jit(solution)/shard_map/ppermute | solution.py:26
  278.0 30.3 %collective-permute-start.10 = (f32[16,64,128]{2,1,0:T(8,128)}, f32[16,64,128]{2,1,0:T(8,128)S(1)}, u32[]{:S(2)}, u32[]{:S(2)}) collective-permute-start(f32[16,64,128]{2,1,0:T(8,128)} %multiply_add_fusion.2), channel_id=1, source_target_pairs={{0,32},{2,34},{4,36},{6,38},{8,40},{10,42},{12,44},{14,46},{16,48}... | collective-permute-start | bytes 1572872 | tf_op jit(solution)/shard_map/ppermute | solution.py:26
  279.6 16.3 %collective-permute-start.4 = (f32[16]{0:T(128)S(1)}, f32[16]{0:T(128)S(1)}, u32[]{:S(2)}, u32[]{:S(2)}) collective-permute-start(f32[16]{0:T(128)S(1)} %fusion.92), channel_id=1, source_target_pairs={{0,16},{2,18},{4,20},{6,22},{8,24},{10,26},{12,28},{14,30},{16,32}... | collective-permute-start | bytes 200 | tf_op jit(solution)/shard_map/ppermute | solution.py:26
  308.3 3.8 copy-start.5
  310.4 16.0 %collective-permute-start.11 = (f32[16,64,128]{2,1,0:T(8,128)}, f32[16,64,128]{2,1,0:T(8,128)}, u32[]{:S(2)}, u32[]{:S(2)}) collective-permute-start(f32[16,64,128]{2,1,0:T(8,128)} %multiply_add_fusion.1), channel_id=1, source_target_pairs={{0,64},{2,66},{4,68},{6,70},{8,72},{10,74},{12,76},{14,78},{16,80}... | collective-permute-start | bytes 1572872 | tf_op jit(solution)/shard_map/ppermute | solution.py:26
  314.3 25.9 %copy-start.4 = (f32[16,64,128]{2,1,0:T(8,128)}, f32[16,64,128]{2,1,0:T(8,128)S(1)}, u32[]{:S(2)}) copy-start(f32[16,64,128]{2,1,0:T(8,128)S(1)} %fusion.19) | copy-start | bytes 1572868
  314.3 4.7 %collective-permute-start.5 = (f32[16]{0:T(128)S(1)}, f32[16]{0:T(128)S(1)}, u32[]{:S(2)}, u32[]{:S(2)}) collective-permute-start(f32[16]{0:T(128)S(1)} %fusion.90), channel_id=1, source_target_pairs={{0,32},{2,34},{4,36},{6,38},{8,40},{10,42},{12,44},{14,46},{16,48}... | collective-permute-start | bytes 200 | tf_op jit(solution)/shard_map/ppermute | solution.py:26
  342.4 1.9 copy-start.1
  351.3 1.9 copy-start.1
  360.3 1.9 copy-start.1
  369.2 1.9 copy-start.1
  378.2 1.9 copy-start.1
  387.1 1.9 copy-start.1
  396.0 1.9 copy-start.1
  405.0 1.9 copy-start.1
  413.8 3.3 collective-permute-start.12
